TPU v7x, 256 devices: a whole 4x4x8 slice. The times are simulated.
256 devices in a mesh: row: 32 (over y, z_hi, x), col: 8 (over z_lo, core).
Axes of the slice: x: 4, y: 4, z: 8 (z_hi: 2, z_lo: 4; z = z_hi * 4 + z_lo), core: 2. Of those that a mesh axis runs over, the one named last changes fastest.
Arguments:
- trailing: float32 [2, 32768, 4096], P(None, 'row', 'col'), may hold values from -6 to 6
- panel: float32 [2, 32768, 256], P(None, ('row', 'col')), may hold values from -4 to 4
- diag_inverse: float32 [2, 256, 256], replicated, as said below
Outputs:
- scaled: float32 [2, 32768, 256], P(None, ('row', 'col'))
- updated: float32 [2, 32768, 4096], P(None, 'row', 'col')
Inputs may be any that keep to these rules, and one draw needn't show every extreme that they name: diag_inverse is complex-symmetric: each part equals its own transpose.
All inputs are finite; a program needn't handle non-finite values.
Results may differ from a plain program's by a relative error of at most 0.00007.
Values sent between devices are 32-bit elements; how exact they have to be, the bound alone decides.
No kernel may reach another device: no remote copies, remote signals or barrier semaphores. Data moves between devices by JAX's collectives and lax.ppermute only.
A program may use at most 64 MiB of HBM per device.

v0:
```python
import jax
import jax.numpy as jnp
from jax import lax
from jax.sharding import Mesh
from jax.sharding import PartitionSpec as P

AXES = ("y", "zh", "x", "zl", "core")
ROW = ("y", "zh", "x")
COL = ("zl", "core")


def complex_product(left, right):
    hp = lax.Precision.HIGHEST
    real_part = jnp.dot(left[0], right[0], precision=hp) - jnp.dot(left[1], right[1], precision=hp)
    imag_part = jnp.dot(left[0], right[1], precision=hp) + jnp.dot(left[1], right[0], precision=hp)
    return jnp.stack([real_part, imag_part])


def product_transposed(left, right):
    hp = lax.Precision.HIGHEST
    dims = (((1,), (1,)), ((), ()))
    real_part = lax.dot_general(left[0], right[0], dims, precision=hp) - lax.dot_general(
        left[1], right[1], dims, precision=hp
    )
    imag_part = lax.dot_general(left[0], right[1], dims, precision=hp) + lax.dot_general(
        left[1], right[0], dims, precision=hp
    )
    return jnp.stack([real_part, imag_part])


def make_local(sizes):
    ny, nh, nx, nl, nc = sizes

    def lin(y, h, x, l, c):
        return (((y * nh + h) * nx + x) * nl + l) * nc + c

    pieces = nl * nc
    transpose = []
    for g in range(nx):
        for l in range(nl):
            for c in range(nc):
                p = nc * l + c
                transpose.append((lin(0, 0, g, l, c), lin(0, 0, p % nx, g, p // nx)))

    def shift(y0, y1, h0, h1):
        return [
            (lin(y0, h0, x, l, c), lin(y1, h1, x, l, c))
            for x in range(nx)
            for l in range(nl)
            for c in range(nc)
        ]

    def local(trailing, panel, diag_inverse):
        scaled = complex_product(panel, diag_inverse)
        block = lax.all_gather(panel, COL, axis=1, tiled=True)
        yi = lax.axis_index("y")
        hi = lax.axis_index("zh")
        piece = lax.ppermute(panel, AXES, transpose)
        r1 = lax.ppermute(piece, AXES, shift(0, 1, 0, 0))
        r3 = lax.ppermute(piece, AXES, shift(0, ny - 1, 0, 0))
        r2 = lax.ppermute(r1, AXES, shift(1, 2, 0, 0))
        along_y = jnp.where(yi == 1, r1, jnp.where(yi == 2, r2, jnp.where(yi == ny - 1, r3, piece)))
        rz = lax.ppermute(along_y, AXES, [pr for y in range(ny) for pr in shift(y, y, 0, 1)])
        held = jnp.where(hi == 0, along_y, rz)
        window = lax.all_gather(held, "x", axis=1, tiled=True)
        tiles = complex_product(window, diag_inverse)
        updated = trailing - product_transposed(block, tiles)
        return (scaled, updated)

    return local


def solution(mesh):
    ny, nh, nx = (4, 2, 4)
    nl, nc = (4, 2)
    devices = mesh.devices.reshape(ny, nh, nx, nl, nc)
    fine = Mesh(devices, AXES)
    return jax.shard_map(
        make_local((ny, nh, nx, nl, nc)),
        mesh=fine,
        in_specs=(P(None, ROW, COL), P(None, ROW + COL, None), P()),
        out_specs=(P(None, ROW + COL, None), P(None, ROW, COL)),
        check_vma=False,
    )
```

profile of v0, /device:TPU:2, one launch (start us, length us, event | category | flops | bytes accessed | tf_op | source)
XLA Modules:
  0.0 150.6 jit_solution(12657731391345822271)
XLA Ops:
  7.2 3.8 %collective-permute-start = (f32[2,128,256]{2,1,0:T(8,128)}, f32[2,128,256]{2,1,0:T(8,128)S(1)}, u32[]{:S(2)}, u32[]{:S(2)}) collective-permute-start(f32[2,128,256]{2,1,0:T(8,128)} %param.4), channel_id=1, source_target_pairs={{0,0},{1,8},{2,16},{3,24},{4,1},{5,9},{6,17},{7,25},{8,2},{9,10},{... | collective-permute-start | bytes 786440 | tf_op jit(solution)/shard_map/ppermute | solution.py:58
  11.0 6.4 %collective-permute-done = f32[2,128,256]{2,1,0:T(8,128)S(1)} collective-permute-done((f32[2,128,256]{2,1,0:T(8,128)}, f32[2,128,256]{2,1,0:T(8,128)S(1)}, u32[]{:S(2)}, u32[]{:S(2)}) %collective-permute-start) | collective-permute-done | bytes 262176 | tf_op jit(solution)/shard_map/ppermute | solution.py:58
  17.5 1.3 collective-permute-start.1
  18.8 1.3 collective-permute-start.3
  20.1 2.5 %collective-permute-done.1 = f32[2,128,256]{2,1,0:T(8,128)S(1)} collective-permute-done((f32[2,128,256]{2,1,0:T(8,128)S(1)}, f32[2,128,256]{2,1,0:T(8,128)S(1)}, u32[]{:S(2)}, u32[]{:S(2)}) %collective-permute-start.1) | collective-permute-done | bytes 262176 | tf_op jit(solution)/shard_map/ppermute | solution.py:59
  22.6 0.7 collective-permute-start.2
  23.3 0.6 collective-permute-done.3
  24.0 1.3 collective-permute-start.4
  25.3 3.9 %collective-permute-done.4 = f32[2,128,256]{2,1,0:T(8,128)S(1)} collective-permute-done((f32[2,128,256]{2,1,0:T(8,128)S(1)}, f32[2,128,256]{2,1,0:T(8,128)S(1)}, u32[]{:S(2)}, u32[]{:S(2)}) %collective-permute-start.4) | collective-permute-done | bytes 262176 | tf_op jit(solution)/shard_map/ppermute | solution.py:63
  29.2 0.7 broadcast_select_fusion
  30.0 0.7 all-gather.5.cloned.1.call-update
  30.7 5.4 %copy.5 = f32[2,1024,512]{1,2,0:T(8,128)} copy(f32[2,1024,512]{2,1,0:T(8,128)} %param.3) | data formatting | bytes 8388608 | tf_op args[0]
  37.3 0.7 pad_maximum_fusion
  38.0 45.9 %all-gather.3.cloned.1.call-done = f32[2,512,256]{2,1,0:T(8,128)} async-done(((f32[2,128,256]{2,1,0:T(8,128)}), f32[2,512,256]{2,1,0:T(8,128)}) %all-gather.3.cloned.1.call-update) | async-done | bytes 1048592 | tf_op jit(solution)/shard_map/all_gather | solution.py:65
  84.0 1.7 %fusion.5 = f32[512,256]{1,0:T(8,128)S(1)} fusion(f32[2,512,256]{2,1,0:T(8,128)} %all-gather.3.cloned.1.call-done, f32[2,256,256]{2,1,0:T(8,128)S(1)} %copy-done.1), kind=kOutput, calls=%fused_computation.16 | convolution fusion | flops 402653184 | bytes 1310720 | tf_op jit(solution)/shard_map/dot_general | solution.py:14
  85.7 1.6 %fusion.4 = f32[512,256]{1,0:T(8,128)S(1)} fusion(f32[2,512,256]{2,1,0:T(8,128)} %all-gather.3.cloned.1.call-done, f32[2,256,256]{2,1,0:T(8,128)S(1)} %copy-done.1), kind=kOutput, calls=%fused_computation.15 | convolution fusion | flops 402653184 | bytes 1310720 | tf_op jit(solution)/shard_map/dot_general | solution.py:15
  87.3 0.6 convolution_subtract_fusion
  88.5 37.6 %all-gather.5.cloned.1.call-done = f32[2,1024,256]{2,1,0:T(8,128)} async-done(((f32[2,128,256]{2,1,0:T(8,128)}), f32[2,1024,256]{2,1,0:T(8,128)}) %all-gather.5.cloned.1.call-update) | async-done | bytes 2097168 | tf_op jit(solution)/shard_map/all_gather | solution.py:55
  126.1 3.2 %fusion.3 = f32[512,1024]{1,0:T(8,128)S(1)} fusion(f32[512,256]{1,0:T(8,128)S(1)} %convolution_subtract_fusion, f32[2,1024,256]{2,1,0:T(8,128)} %all-gather.5.cloned.1.call-done), kind=kOutput, calls=%fused_computation.12 | convolution fusion | flops 1610612736 | bytes 3670016 | tf_op jit(solution)/shard_map/dot_general | solution.py:22
  129.4 1.9 %fusion.2 = f32[512,1024]{1,0:T(8,128)S(1)} fusion(f32[512,256]{1,0:T(8,128)S(1)} %convolution_add_fusion, f32[2,1024,256]{2,1,0:T(8,128)S(1)} %copy-done.2), kind=kOutput, calls=%fused_computation.11 | convolution fusion | flops 1610612736 | bytes 3670016 | tf_op jit(solution)/shard_map/dot_general | solution.py:25
  131.3 2.0 %subtract_bitcast_fusion = f32[1,1024,512]{1,2,0:T(8,128)S(1)} fusion(f32[512,1024]{1,0:T(8,128)S(1)} %fusion.3, f32[512,256]{1,0:T(8,128)S(1)} %convolution_add_fusion, f32[2,1024,256]{2,1,0:T(8,128)S(1)} %copy-done.2), kind=kOutput, calls=%fused_computation.2 | convolution fusion | flops 1611137024 | bytes 5767168 | tf_op jit(solution)/shard_map/dot_general | solution.py:22
  133.3 2.0 %add_bitcast_fusion = f32[1,1024,512]{1,2,0:T(8,128)S(1)} fusion(f32[512,1024]{1,0:T(8,128)S(1)} %fusion.2, f32[512,256]{1,0:T(8,128)S(1)} %convolution_subtract_fusion, f32[2,1024,256]{2,1,0:T(8,128)S(1)} %copy-done.2), kind=kOutput, calls=%fused_computation.1 | convolution fusion | flops 1611137024 | bytes 5767168 | tf_op jit(solution)/shard_map/dot_general | solution.py:25
  135.5 2.9 %maximum_subtract_fusion = f32[2,1024,512]{1,2,0:T(8,128)} fusion(f32[2,1024,512]{1,2,0:T(8,128)S(1)} %copy-done, f32[1,1024,512]{1,2,0:T(8,128)S(1)} %add_bitcast_fusion, f32[1,1024,512]{1,2,0:T(8,128)S(1)} %subtract_bitcast_fusion), kind=kLoop, calls=%fused_computation | loop fusion | flops 2097152 | bytes 12582912 | tf_op jit(solution)/shard_map/sub | solution.py:67
  138.4 5.4 %copy.6 = f32[2,1024,512]{2,1,0:T(8,128)} copy(f32[2,1024,512]{1,2,0:T(8,128)} %maximum_subtract_fusion) | data formatting | bytes 8388608
  (20 shorter events, 2.1 us)
Async XLA Ops:
  7.2 76.8 %all-gather.3.cloned.1.call-start = ((), (), s32[]{:S(2)}) async-start(), calls=%async_computation | async-start | bytes 1310720 | tf_op jit(solution)/shard_map/all_gather | solution.py:65
  7.2 10.3 %collective-permute-start = (f32[2,128,256]{2,1,0:T(8,128)}, f32[2,128,256]{2,1,0:T(8,128)S(1)}, u32[]{:S(2)}, u32[]{:S(2)}) collective-permute-start(f32[2,128,256]{2,1,0:T(8,128)} %param.4), channel_id=1, source_target_pairs={{0,0},{1,8},{2,16},{3,24},{4,1},{5,9},{6,17},{7,25},{8,2},{9,10},{... | collective-permute-start | bytes 786440 | tf_op jit(solution)/shard_map/ppermute | solution.py:58
  17.5 5.2 %collective-permute-start.1 = (f32[2,128,256]{2,1,0:T(8,128)S(1)}, f32[2,128,256]{2,1,0:T(8,128)S(1)}, u32[]{:S(2)}, u32[]{:S(2)}) collective-permute-start(f32[2,128,256]{2,1,0:T(8,128)S(1)} %collective-permute-done), channel_id=1, source_target_pairs={{0,64},{1,65},{2,66},{3,67},{4,68},{5,69},{6,70},{7,71},{8,72},{9,... | collective-permute-start | bytes 786440 | tf_op jit(solution)/shard_map/ppermute | solution.py:59
  18.8 5.2 %collective-permute-start.3 = (f32[2,128,256]{2,1,0:T(8,128)S(1)}, f32[2,128,256]{2,1,0:T(8,128)S(1)}, u32[]{:S(2)}, u32[]{:S(2)}) collective-permute-start(f32[2,128,256]{2,1,0:T(8,128)S(1)} %collective-permute-done), channel_id=1, source_target_pairs={{0,192},{1,193},{2,194},{3,195},{4,196},{5,197},{6,198},{7,199},{8... | collective-permute-start | bytes 786440 | tf_op jit(solution)/shard_map/ppermute | solution.py:60
  22.6 1.3 collective-permute-start.2
  24.0 5.2 %collective-permute-start.4 = (f32[2,128,256]{2,1,0:T(8,128)S(1)}, f32[2,128,256]{2,1,0:T(8,128)S(1)}, u32[]{:S(2)}, u32[]{:S(2)}) collective-permute-start(f32[2,128,256]{2,1,0:T(8,128)S(1)} %select_select_fusion), channel_id=1, source_target_pairs={{0,32},{1,33},{2,34},{3,35},{4,36},{5,37},{6,38},{7,39},{8,40},{9,... | collective-permute-start | bytes 786440 | tf_op jit(solution)/shard_map/ppermute | solution.py:63
  29.9 96.2 %all-gather.5.cloned.1.call-start = ((), (), s32[]{:S(2)}) async-start(), calls=%async_computation.1 | async-start | bytes 2359296 | tf_op jit(solution)/shard_map/all_gather | solution.py:55
  30.7 5.5 %copy-start.1 = (f32[2,256,256]{2,1,0:T(8,128)S(1)}, f32[2,256,256]{2,1,0:T(8,128)}, u32[]{:S(2)}) copy-start(f32[2,256,256]{2,1,0:T(8,128)} %param.5) | copy-start | bytes 1572868
  30.7 5.4 %copy-start.4 = (f32[2,128,256]{2,1,0:T(8,128)S(1)}, f32[2,128,256]{2,1,0:T(8,128)}, u32[]{:S(2)}) copy-start(f32[2,128,256]{2,1,0:T(8,128)} %param.4) | copy-start | bytes 786436
  84.0 3.3 %copy-start.3 = (f32[2,512,256]{2,1,0:T(8,128)S(1)}, f32[2,512,256]{2,1,0:T(8,128)}, u32[]{:S(2)}) copy-start(f32[2,512,256]{2,1,0:T(8,128)} %all-gather.3.cloned.1.call-done) | copy-start | bytes 3145732
  126.1 3.2 %copy-start.2 = (f32[2,1024,256]{2,1,0:T(8,128)S(1)}, f32[2,1024,256]{2,1,0:T(8,128)}, u32[]{:S(2)}) copy-start(f32[2,1024,256]{2,1,0:T(8,128)} %all-gather.5.cloned.1.call-done) | copy-start | bytes 6291460
  133.3 2.2 %copy-start = (f32[2,1024,512]{1,2,0:T(8,128)S(1)}, f32[2,1024,512]{1,2,0:T(8,128)}, u32[]{:S(2)}) copy-start(f32[2,1024,512]{1,2,0:T(8,128)} %copy.5) | copy-start | bytes 12582916
Sparse Core Ops, SparseCore 0:
  30.1 53.8 all-gather.2
  85.8 40.3 all-gather.4
where the time goes:
time: 151 us
  waiting for transfers between devices  97.7 us (65%)
  matrix products  14.7 us (10%)
  between operations  14.2 us (9%)
  local copies, waits for them, and re-layouts  11 us (7%)
  starting transfers between devices  8.45 us (6%)
  other arithmetic  4.41 us (3%)
    all_gather x1, waiting for transfers between devices, local(): window = lax.all_gather(held, 'x', axis=1, tiled=True)  45.9 us
    all_gather x1, waiting for transfers between devices, local(): block = lax.all_gather(panel, COL, axis=1, tiled=True)  37.6 us
    unnamed x12, local copies, waits for them, and re-layouts  11 us
    ppermute x1, waiting for transfers between devices, local(): piece = lax.ppermute(panel, AXES, transpose)  6.45 us
    ppermute x1, waiting for transfers between devices, local(): lax.ppermute(along_y, AXES, [pr for y in range(ny) for pr in shift(y, y,...  3.85 us
    ppermute x1, starting transfers between devices, local(): piece = lax.ppermute(panel, AXES, transpose)  3.8 us
    dot_general x1, matrix products, product_transposed(): lax.dot_general(left[0], right[0], dims, precision=hp)  3.24 us
  transfers between devices with their start and end apart: 7, of which 6 were waited for; matrix products, arithmetic and copies ran while one was open for 8% of the time, Pallas kernels for 0%

commit v1 on v0

--- a/solution.py
+++ b/solution.py
@@ -7,6 +7,11 @@
 AXES = ("y", "zh", "x", "zl", "core")
 ROW = ("y", "zh", "x")
 COL = ("zl", "core")
+
+
+def gather_over(block, axis, d):
+    sent = jnp.stack([block] * lax.axis_size(axis))
+    return jnp.concatenate(lax.all_to_all(sent, axis, 0, 0), axis=d)
 
 
 def complex_product(left, right):
@@ -52,7 +57,7 @@
 
     def local(trailing, panel, diag_inverse):
         scaled = complex_product(panel, diag_inverse)
-        block = lax.all_gather(panel, COL, axis=1, tiled=True)
+        block = gather_over(panel, COL, 1)
         yi = lax.axis_index("y")
         hi = lax.axis_index("zh")
         piece = lax.ppermute(panel, AXES, transpose)

time: 151 us -> 135 us (0.89)
  waiting for transfers between devices: 97.7 us -> 60.1 us
  starting transfers between devices: 8.45 us -> 26.9 us
  local copies, waits for them, and re-layouts: 11 us -> 13.7 us
    all_gather x1 -> x0, waiting for transfers between devices: 37.6 us -> none  [local(): block = lax.all_gather(panel, COL, axis=1, tiled=True)]
    all_gather x1, waiting for transfers between devices: 45.9 us -> 16.6 us  [local(): window = lax.all_gather(held, 'x', axis=1, tiled=True)]
    ppermute x1, waiting for transfers between devices: 3.85 us -> 31.3 us  [local(): lax.ppermute(along_y, AXES, [pr for y in range(ny) for pr in shift(y, y,...]
    all_to_all x0 -> x1, starting transfers between devices: none -> 18.5 us  [gather_over(): return jnp.concatenate(lax.all_to_all(sent, axis, 0, 0), axis=d)]
    ppermute x1, waiting for transfers between devices: 0.63 us -> 5.72 us  [local(): r3 = lax.ppermute(piece, AXES, shift(0, ny - 1, 0, 0))]
    ppermute x1, waiting for transfers between devices: 2.54 us -> 0.01 us  [local(): r1 = lax.ppermute(piece, AXES, shift(0, 1, 0, 0))]
    another operation x0 -> x1, local copies, waits for them, and re-layouts: none -> 2.49 us  [gather_over(): sent = jnp.stack([block] * lax.axis_size(axis))]
  transfers between devices with their start and end apart: 7 -> 7, of which waited for: 6 -> 4; matrix products, arithmetic and copies ran while one was open for 8% -> 12% of each run, Pallas kernels for 0% -> 0%
where the time goes in v1:
time: 135 us; the launch traced here: 133 us
  waiting for transfers between devices  60.1 us (45%)
  starting transfers between devices  26.9 us (20%)
  between operations  14.2 us (11%)
  matrix products  14.1 us (10%)
  local copies, waits for them, and re-layouts  13.7 us (10%)
  other arithmetic  4.41 us (3%)
    ppermute x1, waiting for transfers between devices, local(): lax.ppermute(along_y, AXES, [pr for y in range(ny) for pr in shift(y, y,...  31.3 us
    all_to_all x1, starting transfers between devices, gather_over(): return jnp.concatenate(lax.all_to_all(sent, axis, 0, 0), axis=d)  18.5 us
    all_gather x1, waiting for transfers between devices, local(): window = lax.all_gather(held, 'x', axis=1, tiled=True)  16.6 us
    unnamed x12, local copies, waits for them, and re-layouts  11 us
    ppermute x1, waiting for transfers between devices, local(): piece = lax.ppermute(panel, AXES, transpose)  6.45 us
    ppermute x1, waiting for transfers between devices, local(): r3 = lax.ppermute(piece, AXES, shift(0, ny - 1, 0, 0))  5.72 us
    ppermute x1, starting transfers between devices, local(): piece = lax.ppermute(panel, AXES, transpose)  3.8 us
    sub x1, other arithmetic, local(): updated = trailing - product_transposed(block, tiles)  2.89 us
  transfers between devices with their start and end apart: 7, of which 4 were waited for; matrix products, arithmetic and copies ran while one was open for 12% of the time, Pallas kernels for 0%

profile of v1, /device:TPU:2, one launch (start us, length us, event | category | flops | bytes accessed | tf_op | source)
XLA Modules:
  0.0 133.4 jit_solution(4554178497953800075)
XLA Ops:
  7.2 3.8 %collective-permute-start = (f32[2,128,256]{2,1,0:T(8,128)}, f32[2,128,256]{2,1,0:T(8,128)S(1)}, u32[]{:S(2)}, u32[]{:S(2)}) collective-permute-start(f32[2,128,256]{2,1,0:T(8,128)} %param.4), channel_id=1, source_target_pairs={{0,0},{1,8},{2,16},{3,24},{4,1},{5,9},{6,17},{7,25},{8,2},{9,10},{... | collective-permute-start | bytes 786440 | tf_op jit(solution)/shard_map/ppermute | solution.py:63
  11.0 6.4 %collective-permute-done = f32[2,128,256]{2,1,0:T(8,128)S(1)} collective-permute-done((f32[2,128,256]{2,1,0:T(8,128)}, f32[2,128,256]{2,1,0:T(8,128)S(1)}, u32[]{:S(2)}, u32[]{:S(2)}) %collective-permute-start) | collective-permute-done | bytes 262176 | tf_op jit(solution)/shard_map/ppermute | solution.py:63
  17.4 1.3 collective-permute-start.1
  18.7 2.5 %stack.32 = f32[8,2,128,256]{3,2,1,0:T(8,128)} broadcast(f32[2,128,256]{2,1,0:T(8,128)} %param.4), dimensions={1,2,3} | broadcast | bytes 2359296 | tf_op jit(solution)/shard_map/stack | solution.py:13
  21.2 18.5 %all-to-all-start = ((f32[8,2,128,256]{3,2,1,0:T(8,128)}), f32[8,2,128,256]{3,2,1,0:T(8,128)S(1)}, u32[]{:S(2)}, u32[]{:S(2)}) async-start(f32[8,2,128,256]{3,2,1,0:T(8,128)} %stack.32), calls=%async_computation | async-start | bytes 4194304 | tf_op jit(solution)/shard_map/all_to_all | solution.py:14
  39.8 1.3 collective-permute-start.3
  41.1 0.7 collective-permute-start.2
  41.8 5.7 %collective-permute-done.3 = f32[2,128,256]{2,1,0:T(8,128)S(1)} collective-permute-done((f32[2,128,256]{2,1,0:T(8,128)S(1)}, f32[2,128,256]{2,1,0:T(8,128)S(1)}, u32[]{:S(2)}, u32[]{:S(2)}) %collective-permute-start.3) | collective-permute-done | bytes 262176 | tf_op jit(solution)/shard_map/ppermute | solution.py:65
  47.6 1.3 collective-permute-start.4
  48.9 31.3 %collective-permute-done.4 = f32[2,128,256]{2,1,0:T(8,128)S(1)} collective-permute-done((f32[2,128,256]{2,1,0:T(8,128)S(1)}, f32[2,128,256]{2,1,0:T(8,128)S(1)}, u32[]{:S(2)}, u32[]{:S(2)}) %collective-permute-start.4) | collective-permute-done | bytes 262176 | tf_op jit(solution)/shard_map/ppermute | solution.py:68
  80.2 0.7 broadcast_select_fusion
  81.0 5.4 %copy.5 = f32[2,1024,512]{1,2,0:T(8,128)} copy(f32[2,1024,512]{2,1,0:T(8,128)} %param.3) | data formatting | bytes 8388608 | tf_op args[0]
  87.6 0.7 pad_maximum_fusion
  88.3 16.6 %all-gather.2.cloned.1.call-done = f32[2,512,256]{2,1,0:T(8,128)} async-done(((f32[2,128,256]{2,1,0:T(8,128)}), f32[2,512,256]{2,1,0:T(8,128)}) %all-gather.2.cloned.1.call-update) | async-done | bytes 1048592 | tf_op jit(solution)/shard_map/all_gather | solution.py:70
  104.9 1.7 %fusion.3 = f32[512,256]{1,0:T(8,128)S(1)} fusion(f32[2,512,256]{2,1,0:T(8,128)} %all-gather.2.cloned.1.call-done, f32[2,256,256]{2,1,0:T(8,128)S(1)} %copy-done.1), kind=kOutput, calls=%fused_computation.12 | convolution fusion | flops 402653184 | bytes 1310720 | tf_op jit(solution)/shard_map/dot_general | solution.py:19
  106.6 1.6 %fusion.2 = f32[512,256]{1,0:T(8,128)S(1)} fusion(f32[2,512,256]{2,1,0:T(8,128)} %all-gather.2.cloned.1.call-done, f32[2,256,256]{2,1,0:T(8,128)S(1)} %copy-done.1), kind=kOutput, calls=%fused_computation.11 | convolution fusion | flops 402653184 | bytes 1310720 | tf_op jit(solution)/shard_map/dot_general | solution.py:20
  108.2 0.6 convolution_subtract_fusion
  108.8 1.4 %convolution_add_fusion = f32[512,256]{1,0:T(8,128)} fusion(f32[512,256]{1,0:T(8,128)S(1)} %fusion.2, f32[2,512,256]{2,1,0:T(8,128)S(1)} %copy-done.3, f32[2,256,256]{2,1,0:T(8,128)S(1)} %copy-done.1), kind=kOutput, calls=%fused_computation.3 | convolution fusion | flops 402784256 | bytes 1835008 | tf_op jit(solution)/shard_map/dot_general | solution.py:20
  110.4 1.9 %fusion.31 = f32[512,1024]{1,0:T(8,128)S(1)} fusion(f32[512,256]{1,0:T(8,128)S(1)} %convolution_subtract_fusion, f32[1024,256]{1,0:T(8,128)S(1)} %bitcast.59), kind=kOutput, calls=%fused_computation.43 | convolution fusion | flops 1610612736 | bytes 3670016 | tf_op jit(solution)/shard_map/dot_general | solution.py:27
  112.2 1.9 %fusion.32 = f32[512,1024]{1,0:T(8,128)S(1)} fusion(f32[512,256]{1,0:T(8,128)S(1)} %copy-done.2, f32[1024,256]{1,0:T(8,128)S(1)} %bitcast.60), kind=kOutput, calls=%fused_computation.44 | convolution fusion | flops 1610612736 | bytes 3670016 | tf_op jit(solution)/shard_map/dot_general | solution.py:30
  114.1 2.0 %subtract_bitcast_fusion = f32[1,1024,512]{1,2,0:T(8,128)S(1)} fusion(f32[512,1024]{1,0:T(8,128)S(1)} %fusion.31, f32[512,256]{1,0:T(8,128)S(1)} %copy-done.2, f32[1024,256]{1,0:T(8,128)S(1)} %bitcast.61), kind=kOutput, calls=%fused_computation.2 | convolution fusion | flops 1611137024 | bytes 5767168 | tf_op jit(solution)/shard_map/dot_general | solution.py:27
  116.1 2.0 %add_bitcast_fusion = f32[1,1024,512]{1,2,0:T(8,128)S(1)} fusion(f32[512,1024]{1,0:T(8,128)S(1)} %fusion.32, f32[512,256]{1,0:T(8,128)S(1)} %convolution_subtract_fusion, f32[1024,256]{1,0:T(8,128)S(1)} %bitcast.62), kind=kOutput, calls=%fused_computation.1 | convolution fusion | flops 1611137024 | bytes 5767168 | tf_op jit(solution)/shard_map/dot_general | solution.py:30
  118.3 2.9 %maximum_subtract_fusion = f32[2,1024,512]{1,2,0:T(8,128)} fusion(f32[2,1024,512]{1,2,0:T(8,128)S(1)} %copy-done, f32[1,1024,512]{1,2,0:T(8,128)S(1)} %add_bitcast_fusion, f32[1,1024,512]{1,2,0:T(8,128)S(1)} %subtract_bitcast_fusion), kind=kLoop, calls=%fused_computation | loop fusion | flops 2097152 | bytes 12582912 | tf_op jit(solution)/shard_map/sub | solution.py:72
  121.2 5.4 %copy.6 = f32[2,1024,512]{2,1,0:T(8,128)} copy(f32[2,1024,512]{1,2,0:T(8,128)} %maximum_subtract_fusion) | data formatting | bytes 8388608
  (21 shorter events, 1.6 us)
Async XLA Ops:
  7.2 10.3 %collective-permute-start = (f32[2,128,256]{2,1,0:T(8,128)}, f32[2,128,256]{2,1,0:T(8,128)S(1)}, u32[]{:S(2)}, u32[]{:S(2)}) collective-permute-start(f32[2,128,256]{2,1,0:T(8,128)} %param.4), channel_id=1, source_target_pairs={{0,0},{1,8},{2,16},{3,24},{4,1},{5,9},{6,17},{7,25},{8,2},{9,10},{... | collective-permute-start | bytes 786440 | tf_op jit(solution)/shard_map/ppermute | solution.py:63
  17.4 23.7 %collective-permute-start.1 = (f32[2,128,256]{2,1,0:T(8,128)S(1)}, f32[2,128,256]{2,1,0:T(8,128)S(1)}, u32[]{:S(2)}, u32[]{:S(2)}) collective-permute-start(f32[2,128,256]{2,1,0:T(8,128)S(1)} %collective-permute-done), channel_id=1, source_target_pairs={{0,64},{1,65},{2,66},{3,67},{4,68},{5,69},{6,70},{7,71},{8,72},{9,... | collective-permute-start | bytes 786440 | tf_op jit(solution)/shard_map/ppermute | solution.py:64
  21.2 89.0 %all-to-all-start = ((f32[8,2,128,256]{3,2,1,0:T(8,128)}), f32[8,2,128,256]{3,2,1,0:T(8,128)S(1)}, u32[]{:S(2)}, u32[]{:S(2)}) async-start(f32[8,2,128,256]{3,2,1,0:T(8,128)} %stack.32), calls=%async_computation | async-start | bytes 4194304 | tf_op jit(solution)/shard_map/all_to_all | solution.py:14
  39.7 65.1 %all-gather.2.cloned.1.call-start = ((), (), s32[]{:S(2)}) async-start(), calls=%async_computation.1 | async-start | bytes 1310720 | tf_op jit(solution)/shard_map/all_gather | solution.py:70
  39.8 7.7 %collective-permute-start.3 = (f32[2,128,256]{2,1,0:T(8,128)S(1)}, f32[2,128,256]{2,1,0:T(8,128)S(1)}, u32[]{:S(2)}, u32[]{:S(2)}) collective-permute-start(f32[2,128,256]{2,1,0:T(8,128)S(1)} %collective-permute-done), channel_id=1, source_target_pairs={{0,192},{1,193},{2,194},{3,195},{4,196},{5,197},{6,198},{7,199},{8... | collective-permute-start | bytes 786440 | tf_op jit(solution)/shard_map/ppermute | solution.py:65
  41.1 6.4 %collective-permute-start.2 = (f32[2,128,256]{2,1,0:T(8,128)S(1)}, f32[2,128,256]{2,1,0:T(8,128)S(1)}, u32[]{:S(2)}, u32[]{:S(2)}) collective-permute-start(f32[2,128,256]{2,1,0:T(8,128)S(1)} %collective-permute-done.1), channel_id=1, source_target_pairs={{64,128},{65,129},{66,130},{67,131},{68,132},{69,133},{70,134},{71... | collective-permute-start | bytes 786440 | tf_op jit(solution)/shard_map/ppermute | solution.py:66
  47.6 32.6 %collective-permute-start.4 = (f32[2,128,256]{2,1,0:T(8,128)S(1)}, f32[2,128,256]{2,1,0:T(8,128)S(1)}, u32[]{:S(2)}, u32[]{:S(2)}) collective-permute-start(f32[2,128,256]{2,1,0:T(8,128)S(1)} %select_select_fusion), channel_id=1, source_target_pairs={{0,32},{1,33},{2,34},{3,35},{4,36},{5,37},{6,38},{7,39},{8,40},{9,... | collective-permute-start | bytes 786440 | tf_op jit(solution)/shard_map/ppermute | solution.py:68
  81.0 5.5 %copy-start.1 = (f32[2,256,256]{2,1,0:T(8,128)S(1)}, f32[2,256,256]{2,1,0:T(8,128)}, u32[]{:S(2)}) copy-start(f32[2,256,256]{2,1,0:T(8,128)} %param.5) | copy-start | bytes 1572868
  81.0 5.4 %copy-start.4 = (f32[2,128,256]{2,1,0:T(8,128)S(1)}, f32[2,128,256]{2,1,0:T(8,128)}, u32[]{:S(2)}) copy-start(f32[2,128,256]{2,1,0:T(8,128)} %param.4) | copy-start | bytes 786436
  104.9 3.3 %copy-start.3 = (f32[2,512,256]{2,1,0:T(8,128)S(1)}, f32[2,512,256]{2,1,0:T(8,128)}, u32[]{:S(2)}) copy-start(f32[2,512,256]{2,1,0:T(8,128)} %all-gather.2.cloned.1.call-done) | copy-start | bytes 3145732
  110.3 1.9 %copy-start.2 = (f32[512,256]{1,0:T(8,128)S(1)}, f32[512,256]{1,0:T(8,128)}, u32[]{:S(2)}) copy-start(f32[512,256]{1,0:T(8,128)} %convolution_add_fusion) | copy-start | bytes 1572868
  116.1 2.2 %copy-start = (f32[2,1024,512]{1,2,0:T(8,128)S(1)}, f32[2,1024,512]{1,2,0:T(8,128)}, u32[]{:S(2)}) copy-start(f32[2,1024,512]{1,2,0:T(8,128)} %copy.5) | copy-start | bytes 12582916
Sparse Core Ops, SparseCore 0:
  81.1 23.7 all-gather.1
